TPU v7x, 32 devices: a whole 2x2x4 slice. The times are simulated.
32 devices in a mesh: grp: 4 (over z), band: 8 (over y, x, core).
Axes of the slice: x: 2, y: 2, z: 4, core: 2. Of those that a mesh axis runs over, the one named last changes fastest.
Arguments:
- orbitals: float32 [18432, 512], P('grp', 'band'), may hold values from -6 to 6
- requests: int32 [32, 6], replicated, may hold values from -1 to 11, as said below
- coulomb: float32 [96, 1536, 1536], P(('grp', 'band')), may hold values from -0.001953125 to 0.001953125
Outputs:
- exchange_rows: float32 [18432, 512], P('grp', 'band')
Inputs may be any that keep to these rules, and one draw needn't show every extreme that they name: `requests`: entries 2q and 2q + 1 of row d are the two blocks of slot q of device d, the first not above the second, or both -1 for an empty slot; every pair of the 12 blocks, a block with itself included, stands in exactly one slot.
All inputs are finite; a program needn't handle non-finite values.
Results may differ from a plain program's by a relative error of at most 0.0003.
Values sent between devices are 32-bit elements; how exact they have to be, the bound alone decides.
No kernel may reach another device: no remote copies, remote signals or barrier semaphores. Data moves between devices by JAX's collectives and lax.ppermute only.
A program may use at most 256 MiB of HBM per device.

v0:
```python
import jax
import jax.numpy as jnp
from jax import lax
from jax.sharding import PartitionSpec as P

PRECISION = lax.Precision.HIGH


def band_exchange(outgoing):
    return lax.all_to_all(outgoing, "band", split_axis=0, concat_axis=0, tiled=True)


def line_gather(x, axis, count, riders=()):
    index = lax.axis_index(axis)
    spare = jnp.zeros((count + 1,) + x.shape, x.dtype)
    spare = lax.dynamic_update_index_in_dim(spare, x, index, 0)
    rightward, leftward = (x, x)
    carried = []
    for step in range(1, count):
        rider = step - 1 < len(riders)
        if rider:
            rightward, leftward, load = lax.optimization_barrier(
                (rightward, leftward, riders[step - 1])
            )
        rightward = lax.ppermute(rightward, axis, [(i, i + 1) for i in range(step - 1, count - 1)])
        leftward = lax.ppermute(leftward, axis, [(i + 1, i) for i in range(0, count - step)])
        if rider:
            rightward, leftward, load = lax.optimization_barrier(
                (rightward, leftward, band_exchange(load))
            )
            carried.append(load)
        from_left = jnp.where(index >= step, index - step, count)
        from_right = jnp.where(index + step < count, index + step, count)
        spare = lax.dynamic_update_index_in_dim(spare, rightward, from_left, 0)
        spare = lax.dynamic_update_index_in_dim(spare, leftward, from_right, 0)
    carried += [band_exchange(load) for load in riders[len(carried) :]]
    return (spare[:count], carried)


def line_reduce(parts, axis, count, riders=()):
    index = lax.axis_index(axis)

    def part_for(target):
        return lax.dynamic_index_in_dim(parts, jnp.clip(target, 0, count - 1), 0, keepdims=False)

    rightward = jnp.zeros(parts.shape[1:], parts.dtype)
    leftward = jnp.zeros(parts.shape[1:], parts.dtype)
    carried = []
    for step in range(1, count):
        send_right = rightward + part_for(index + count - step)
        send_left = leftward + part_for(index - count + step)
        rider = step - 1 < len(riders)
        if rider:
            send_right, send_left, load = lax.optimization_barrier(
                (send_right, send_left, riders[step - 1])
            )
        rightward = lax.ppermute(send_right, axis, [(i, i + 1) for i in range(0, step)])
        leftward = lax.ppermute(send_left, axis, [(i, i - 1) for i in range(count - step, count)])
        if rider:
            rightward, leftward, load = lax.optimization_barrier(
                (rightward, leftward, band_exchange(load))
            )
            carried.append(load)
    carried += [band_exchange(load) for load in riders[len(carried) :]]
    return (part_for(index) + rightward + leftward, carried)


def body(orbitals, requests, coulomb):
    group_count = lax.axis_size("grp")
    band_count = lax.axis_size("band")
    devices = group_count * band_count
    blk = coulomb.shape[1]
    orbital_width = orbitals.shape[1] * band_count
    half = orbital_width // 2
    piece_rows = blk // devices
    slot_count = coulomb.shape[0]
    block_count = orbitals.shape[0] // (band_count * piece_rows)
    col_half = orbitals.shape[1] // 2
    own_rows = [
        lax.all_to_all(
            orbitals[:, h * col_half : (h + 1) * col_half],
            "band",
            split_axis=0,
            concat_axis=1,
            tiled=True,
        )
        for h in range(2)
    ]
    group_index = lax.axis_index("grp")
    band_index = lax.axis_index("band")
    group_requests = lax.dynamic_slice_in_dim(requests, group_index * band_count, band_count, 0)
    own_pairs = lax.dynamic_index_in_dim(group_requests, band_index, 0, keepdims=False)
    one_hot = (
        group_requests[:, :, None] == jnp.arange(block_count, dtype=jnp.int32)[None, None, :]
    ).astype(jnp.float32)

    def requested(pieces, slot):
        wanted = group_requests[:, 2 * slot : 2 * slot + 2]
        wanted = jnp.where(wanted >= 0, wanted, block_count)
        outgoing = jnp.take(pieces, wanted, axis=1, mode="fill", fill_value=0.0)
        return outgoing.transpose(1, 2, 0, 3, 4)

    def shape_pieces(gathered):
        return gathered.reshape(group_count, block_count, piece_rows, half)

    first_pieces = shape_pieces(line_gather(own_rows[0], "grp", group_count)[0])
    first_loads = [requested(first_pieces, slot) for slot in range(slot_count)]
    second_pieces, first_arrived = line_gather(own_rows[1], "grp", group_count, first_loads)
    second_pieces = shape_pieces(second_pieces)
    second_arrived = [band_exchange(requested(second_pieces, slot)) for slot in range(slot_count)]
    returned = [[], []]
    held = []
    for slot in range(slot_count):
        rows = [
            arrived.transpose(1, 2, 0, 3, 4).reshape(2, blk, half)
            for arrived in (first_arrived[slot], second_arrived[slot])
        ]
        density = sum(
            (
                jnp.dot(r[0], r[1].T, precision=PRECISION, preferred_element_type=jnp.float32)
                for r in rows
            )
        )
        scale = jnp.where(own_pairs[2 * slot] == own_pairs[2 * slot + 1], 0.5, 1.0)
        kernel = density * (coulomb[slot] * scale)
        for h in range(2):
            onto_first = jnp.dot(
                kernel, rows[h][1], precision=PRECISION, preferred_element_type=jnp.float32
            )
            onto_second = jnp.dot(
                kernel.T, rows[h][0], precision=PRECISION, preferred_element_type=jnp.float32
            )
            outbound = jnp.stack([onto_first, onto_second], 0).reshape(
                2, group_count, band_count, piece_rows, half
            )
            outbound = outbound.transpose(2, 0, 1, 3, 4)
            if h == 0:
                returned[0].append(band_exchange(outbound))
            else:
                held.append(outbound)

    def sum_blocks(returned):
        gathered = jnp.concatenate(returned, axis=1)
        return jnp.einsum("srk,srgpn->gkpn", one_hot, gathered, precision=PRECISION)

    first_home, second_returned = line_reduce(sum_blocks(returned[0]), "grp", group_count, held)
    second_home, _ = line_reduce(sum_blocks(second_returned), "grp", group_count)
    home = [
        lax.all_to_all(
            rows.reshape(block_count * piece_rows, half),
            "band",
            split_axis=1,
            concat_axis=0,
            tiled=True,
        )
        for rows in (first_home, second_home)
    ]
    return jnp.concatenate(home, axis=1)


def solution(mesh):
    placed = (P("grp", "band"), P(), P(("grp", "band"), None, None))
    return jax.shard_map(
        body, mesh=mesh, in_specs=placed, out_specs=P("grp", "band"), check_vma=False
    )
```

profile of v0, /device:TPU:0, one launch (start us, length us, event | category | flops | bytes accessed | tf_op | source)
XLA Modules:
  0.0 702.9 jit_solution(11223756371621740991)
XLA Ops:
  1.7 16.1 %all_to_all.136 = f32[8,576,32]{1,2,0:T(8,128)S(1)} all-to-all(f32[8,576,32]{1,2,0:T(8,128)S(1)} %copy.177), channel_id=1, replica_groups=mesh['grp'=4,'band'=8] {'band'}, dimensions={0} | all-to-all | bytes 1179648 | tf_op jit(solution)/shard_map/all_to_all | solution.py:80
  44.5 11.7 %collective-permute-done.3 = f32[576,256]{1,0:T(8,128)S(1)} collective-permute-done((f32[576,256]{1,0:T(8,128)}, f32[576,256]{1,0:T(8,128)S(1)}, u32[]{:S(2)}, u32[]{:S(2)}) %collective-permute-start.3) | collective-permute-done | bytes 589856 | tf_op jit(solution)/shard_map/ppermute | solution.py:26
  57.6 13.5 %collective-permute-done.5 = f32[576,256]{1,0:T(8,128)S(1)} collective-permute-done((f32[576,256]{1,0:T(8,128)S(1)}, f32[576,256]{1,0:T(8,128)S(1)}, u32[]{:S(2)}, u32[]{:S(2)}) %collective-permute-start.5) | collective-permute-done | bytes 589856 | tf_op jit(solution)/shard_map/ppermute | solution.py:26
  103.3 16.8 %all-to-all-done.2 = f32[8,2,4,48,256]{4,3,2,1,0:T(8,128)} async-done(((f32[8,2,4,48,256]{4,3,2,1,0:T(8,128)}), f32[8,2,4,48,256]{4,3,2,1,0:T(8,128)}, u32[]{:S(2)}, u32[]{:S(2)}) %all-to-all-start.2) | async-done | bytes 3145760 | tf_op jit(solution)/shard_map/all_to_all | solution.py:10
  136.4 7.2 %collective-permute-done.9 = f32[576,256]{1,0:T(8,128)} collective-permute-done((f32[576,256]{1,0:T(8,128)S(1)}, f32[576,256]{1,0:T(8,128)}, u32[]{:S(2)}, u32[]{:S(2)}) %collective-permute-start.9) | collective-permute-done | bytes 589856 | tf_op jit(solution)/shard_map/ppermute | solution.py:26
  143.7 18.8 %all-to-all-done.3 = f32[8,2,4,48,256]{4,3,2,1,0:T(8,128)} async-done(((f32[8,2,4,48,256]{4,3,2,1,0:T(8,128)}), f32[8,2,4,48,256]{4,3,2,1,0:T(8,128)}, u32[]{:S(2)}, u32[]{:S(2)}) %all-to-all-start.3) | async-done | bytes 3145760 | tf_op jit(solution)/shard_map/all_to_all | solution.py:10
  176.3 11.8 %collective-permute-done.11 = f32[576,256]{1,0:T(8,128)} collective-permute-done((f32[576,256]{1,0:T(8,128)}, f32[576,256]{1,0:T(8,128)}, u32[]{:S(2)}, u32[]{:S(2)}) %collective-permute-start.11) | collective-permute-done | bytes 589856 | tf_op jit(solution)/shard_map/ppermute | solution.py:26
  188.1 15.8 %all-to-all-done.4 = f32[8,2,4,48,256]{4,3,2,1,0:T(8,128)S(1)} async-done(((f32[8,2,4,48,256]{4,3,2,1,0:T(8,128)}), f32[8,2,4,48,256]{4,3,2,1,0:T(8,128)S(1)}, u32[]{:S(2)}, u32[]{:S(2)}) %all-to-all-start.4) | async-done | bytes 3145760 | tf_op jit(solution)/shard_map/all_to_all | solution.py:10
  231.8 26.9 %all-to-all-done.9 = f32[8,2,4,48,256]{4,3,2,1,0:T(8,128)} async-done(((f32[8,2,4,48,256]{4,3,2,1,0:T(8,128)}), f32[8,2,4,48,256]{4,3,2,1,0:T(8,128)}, u32[]{:S(2)}, u32[]{:S(2)}) %all-to-all-start.9) | async-done | bytes 3145760 | tf_op jit(solution)/shard_map/all_to_all | solution.py:10
  265.8 6.5 fusion.44
  311.9 9.6 %fusion = f32[1536,1536]{1,0:T(8,128)} fusion(f32[1536,1536]{1,0:T(8,128)S(1)} %copy-done.5, f32[1536,256]{1,0:T(8,128)S(1)} %bitcast.341, f32[1536,256]{1,0:T(8,128)S(1)} %bitcast.343, f32[3,1536,1536]{2,1,0:T(8,128)} %param.7, f32[]{:T(128)} %bitcast.81), kind=kOutput, calls=%fused_computation.7 | convolution fusion | flops 3630956544 | bytes 31457284 | tf_op jit(solution)/shard_map/dot_general | solution.py:120
  321.5 9.6 %copy.211 = f32[1536,1536]{1,0:T(8,128)} copy(f32[1536,1536]{0,1:T(8,128)} %bitcast.310) | data formatting | bytes 18874368 | tf_op jit(solution)/shard_map/dot_general | solution.py:130
  331.1 7.0 convolution_bitcast_fusion.7
  351.5 12.1 %fusion.2 = f32[1536,1536]{1,0:T(8,128)} fusion(f32[1536,1536]{1,0:T(8,128)} %fusion.44, f32[1536,256]{1,0:T(8,128)S(1)} %bitcast.351, f32[1536,256]{1,0:T(8,128)S(1)} %bitcast.349, f32[3,1536,1536]{2,1,0:T(8,128)} %param.7, f32[]{:T(128)} %bitcast.39), kind=kOutput, calls=%fused_computation.11 | convolution fusion | flops 3630956544 | bytes 31457284 | tf_op jit(solution)/shard_map/dot_general | solution.py:120
  363.6 9.7 %copy.195 = f32[1536,1536]{1,0:T(8,128)} copy(f32[1536,1536]{0,1:T(8,128)} %bitcast.316) | data formatting | bytes 18874368 | tf_op jit(solution)/shard_map/dot_general | solution.py:130
  373.3 7.0 convolution_bitcast_fusion.11
  394.0 11.5 %fusion.1 = f32[1536,1536]{1,0:T(8,128)} fusion(f32[1536,1536]{1,0:T(8,128)} %fusion.45, f32[1536,256]{1,0:T(8,128)S(1)} %bitcast.345, f32[1536,256]{1,0:T(8,128)S(1)} %bitcast.347, f32[3,1536,1536]{2,1,0:T(8,128)} %param.7, f32[]{:T(128)} %bitcast.60), kind=kOutput, calls=%fused_computation.9 | convolution fusion | flops 3630956544 | bytes 31457284 | tf_op jit(solution)/shard_map/dot_general | solution.py:120
  405.4 9.6 %copy.203 = f32[1536,1536]{1,0:T(8,128)} copy(f32[1536,1536]{0,1:T(8,128)} %bitcast.313) | data formatting | bytes 18874368 | tf_op jit(solution)/shard_map/dot_general | solution.py:130
  415.0 7.4 %convolution_bitcast_fusion.9 = f32[1,4,8,48,256]{4,3,2,1,0:T(8,128)S(1)} fusion(f32[4,8,48,1536]{3,2,1,0:T(8,128)} %bitcast.314, f32[1536,256,1,1]{1,0,3,2:T(8,128)} %bitcast.354), kind=kOutput, calls=%fused_computation.47 | convolution fusion | flops 3623878656 | bytes 12582912 | tf_op jit(solution)/shard_map/dot_general | solution.py:127
  434.0 7.4 %convolution_bitcast_fusion.5 = f32[1,4,8,48,256]{4,3,2,1,0:T(8,128)S(1)} fusion(f32[4,8,48,1536]{3,2,1,0:T(8,128)} %bitcast.318, f32[1536,256,1,1]{1,0,3,2:T(8,128)} %bitcast.350), kind=kOutput, calls=%fused_computation.43 | convolution fusion | flops 3623878656 | bytes 12582912 | tf_op jit(solution)/shard_map/dot_general | solution.py:127
  441.4 7.3 %convolution_bitcast_fusion.4 = f32[1,4,8,48,256]{4,3,2,1,0:T(8,128)S(1)} fusion(f32[4,8,48,1536]{3,2,1,0:T(8,128)} %bitcast.327, f32[1536,256,1,1]{1,0,3,2:T(8,128)S(1)} %bitcast.352), kind=kOutput, calls=%fused_computation.42 | convolution fusion | flops 3623878656 | bytes 12582912 | tf_op jit(solution)/shard_map/dot_general | solution.py:130
  461.5 10.4 %all-to-all-done.8 = f32[8,2,4,48,256]{4,3,2,1,0:T(8,128)} async-done(((f32[8,2,4,48,256]{4,3,2,1,0:T(8,128)}), f32[8,2,4,48,256]{4,3,2,1,0:T(8,128)}, u32[]{:S(2)}, u32[]{:S(2)}) %all-to-all-start.8) | async-done | bytes 3145760 | tf_op jit(solution)/shard_map/all_to_all | solution.py:10
  488.2 7.5 %convolution_bitcast_fusion.3 = f32[1,4,8,48,256]{4,3,2,1,0:T(8,128)S(1)} fusion(f32[4,8,48,1536]{3,2,1,0:T(8,128)} %bitcast.315, f32[1536,256,1,1]{1,0,3,2:T(8,128)} %bitcast.348), kind=kOutput, calls=%fused_computation.41 | convolution fusion | flops 3623878656 | bytes 12582912 | tf_op jit(solution)/shard_map/dot_general | solution.py:127
  512.5 13.5 %all-to-all-done.11 = f32[8,2,4,48,256]{4,3,2,1,0:T(8,128)} async-done(((f32[8,2,4,48,256]{4,3,2,1,0:T(8,128)}), f32[8,2,4,48,256]{4,3,2,1,0:T(8,128)}, u32[]{:S(2)}, u32[]{:S(2)}) %all-to-all-start.11) | async-done | bytes 3145760 | tf_op jit(solution)/shard_map/all_to_all | solution.py:10
  536.2 7.0 convolution_bitcast_fusion.1
  553.7 6.4 collective-permute-done.14
  560.1 13.9 %all-to-all-done.12 = f32[8,2,4,48,256]{4,3,2,1,0:T(8,128)} async-done(((f32[8,2,4,48,256]{4,3,2,1,0:T(8,128)}), f32[8,2,4,48,256]{4,3,2,1,0:T(8,128)}, u32[]{:S(2)}, u32[]{:S(2)}) %all-to-all-start.12) | async-done | bytes 3145760 | tf_op jit(solution)/shard_map/all_to_all | solution.py:10
  604.8 16.1 %all-to-all-done.13 = f32[8,2,4,48,256]{4,3,2,1,0:T(8,128)S(1)} async-done(((f32[8,2,4,48,256]{4,3,2,1,0:T(8,128)}), f32[8,2,4,48,256]{4,3,2,1,0:T(8,128)S(1)}, u32[]{:S(2)}, u32[]{:S(2)}) %all-to-all-start.13) | async-done | bytes 3145760 | tf_op jit(solution)/shard_map/all_to_all | solution.py:10
  629.5 8.7 %collective-permute-done.18 = f32[12,48,256]{2,1,0:T(8,128)S(1)} collective-permute-done((f32[12,48,256]{2,1,0:T(8,128)S(1)}, f32[12,48,256]{2,1,0:T(8,128)S(1)}, u32[]{:S(2)}, u32[]{:S(2)}) %collective-permute-start.18) | collective-permute-done | bytes 589856 | tf_op jit(solution)/shard_map/ppermute | solution.py:57
  644.3 7.8 %collective-permute-done.19 = f32[12,48,256]{2,1,0:T(8,128)S(1)} collective-permute-done((f32[12,48,256]{2,1,0:T(8,128)S(1)}, f32[12,48,256]{2,1,0:T(8,128)S(1)}, u32[]{:S(2)}, u32[]{:S(2)}) %collective-permute-start.19) | collective-permute-done | bytes 589856 | tf_op jit(solution)/shard_map/ppermute | solution.py:57
  666.8 8.1 %all-to-all-start.14 = ((f32[576,8,32]{0,2,1:T(8,128)}), f32[576,8,32]{0,2,1:T(8,128)}, u32[]{:S(2)}, u32[]{:S(2)}) async-start(f32[576,8,32]{0,2,1:T(8,128)} %copy.259), calls=%async_computation.14 | async-start | bytes 1310720 | tf_op jit(solution)/shard_map/all_to_all | solution.py:149
  691.4 9.4 %all-to-all-done.15 = f32[576,8,32]{0,2,1:T(8,128)S(1)} async-done(((f32[576,8,32]{0,2,1:T(8,128)}), f32[576,8,32]{0,2,1:T(8,128)S(1)}, u32[]{:S(2)}, u32[]{:S(2)}) %all-to-all-start.15) | async-done | bytes 589856 | tf_op jit(solution)/shard_map/all_to_all | solution.py:149
  (315 shorter events, 345.1 us)
Async XLA Ops:
  18.9 16.2 %collective-permute-start = (f32[576,256]{1,0:T(8,128)}, f32[576,256]{1,0:T(8,128)}, u32[]{:S(2)}, u32[]{:S(2)}) collective-permute-start(f32[576,256]{1,0:T(8,128)} %copy.179), channel_id=1, source_target_pairs={{0,8},{8,16},{16,24},{1,9},{9,17},{17,25},{2,10},{10,18},{18,26},{... | collective-permute-start | bytes 1769480 | tf_op jit(solution)/shard_map/ppermute | solution.py:25
  23.2 16.8 %collective-permute-start.1 = (f32[576,256]{1,0:T(8,128)}, f32[576,256]{1,0:T(8,128)}, u32[]{:S(2)}, u32[]{:S(2)}) collective-permute-start(f32[576,256]{1,0:T(8,128)} %copy.179), channel_id=1, source_target_pairs={{8,0},{16,8},{24,16},{9,1},{17,9},{25,17},{10,2},{18,10},{26,18},{... | collective-permute-start | bytes 1769480 | tf_op jit(solution)/shard_map/ppermute | solution.py:26
  25.6 52.1 %all-to-all-start = ((f32[8,576,32]{1,2,0:T(8,128)}), f32[8,576,32]{1,2,0:T(8,128)S(1)}, u32[]{:S(2)}, u32[]{:S(2)}) async-start(f32[8,576,32]{1,2,0:T(8,128)} %copy.175), calls=%async_computation | async-start | bytes 1310720 | tf_op jit(solution)/shard_map/all_to_all | solution.py:80
  40.0 16.2 %collective-permute-start.3 = (f32[576,256]{1,0:T(8,128)}, f32[576,256]{1,0:T(8,128)S(1)}, u32[]{:S(2)}, u32[]{:S(2)}) collective-permute-start(f32[576,256]{1,0:T(8,128)} %collective-permute-done.1), channel_id=1, source_target_pairs={{8,0},{16,8},{9,1},{17,9},{10,2},{18,10},{11,3},{19,11},{12,4},{20... | collective-permute-start | bytes 1769480 | tf_op jit(solution)/shard_map/ppermute | solution.py:26
  42.7 14.9 %collective-permute-start.4 = (f32[576,256]{1,0:T(8,128)S(1)}, f32[576,256]{1,0:T(8,128)S(1)}, u32[]{:S(2)}, u32[]{:S(2)}) collective-permute-start(f32[576,256]{1,0:T(8,128)S(1)} %collective-permute-done.2), channel_id=1, source_target_pairs={{16,24},{17,25},{18,26},{19,27},{20,28},{21,29},{22,30},{23,31}} | collective-permute-start | bytes 1769480 | tf_op jit(solution)/shard_map/ppermute | solution.py:25
  56.2 14.9 %collective-permute-start.5 = (f32[576,256]{1,0:T(8,128)S(1)}, f32[576,256]{1,0:T(8,128)S(1)}, u32[]{:S(2)}, u32[]{:S(2)}) collective-permute-start(f32[576,256]{1,0:T(8,128)S(1)} %collective-permute-done.3), channel_id=1, source_target_pairs={{8,0},{9,1},{10,2},{11,3},{12,4},{13,5},{14,6},{15,7}} | collective-permute-start | bytes 1769480 | tf_op jit(solution)/shard_map/ppermute | solution.py:26
  77.7 42.4 %all-to-all-start.2 = ((f32[8,2,4,48,256]{4,3,2,1,0:T(8,128)}), f32[8,2,4,48,256]{4,3,2,1,0:T(8,128)}, u32[]{:S(2)}, u32[]{:S(2)}) async-start(f32[8,2,4,48,256]{4,3,2,1,0:T(8,128)} %broadcast_select_fusion.5), calls=%async_computation.2 | async-start | bytes 6291456 | tf_op jit(solution)/shard_map/all_to_all | solution.py:10
  84.3 17.7 %collective-permute-start.7 = (f32[576,256]{1,0:T(8,128)}, f32[576,256]{1,0:T(8,128)S(1)}, u32[]{:S(2)}, u32[]{:S(2)}) collective-permute-start(f32[576,256]{1,0:T(8,128)} %copy.183), channel_id=1, source_target_pairs={{8,0},{16,8},{24,16},{9,1},{17,9},{25,17},{10,2},{18,10},{26,18},{... | collective-permute-start | bytes 1769480 | tf_op jit(solution)/shard_map/ppermute | solution.py:26
  85.6 17.7 %collective-permute-start.6 = (f32[576,256]{1,0:T(8,128)}, f32[576,256]{1,0:T(8,128)S(1)}, u32[]{:S(2)}, u32[]{:S(2)}) collective-permute-start(f32[576,256]{1,0:T(8,128)} %copy.182), channel_id=1, source_target_pairs={{0,8},{8,16},{16,24},{1,9},{9,17},{17,25},{2,10},{10,18},{18,26},{... | collective-permute-start | bytes 1769480 | tf_op jit(solution)/shard_map/ppermute | solution.py:25
  120.1 42.4 %all-to-all-start.3 = ((f32[8,2,4,48,256]{4,3,2,1,0:T(8,128)}), f32[8,2,4,48,256]{4,3,2,1,0:T(8,128)}, u32[]{:S(2)}, u32[]{:S(2)}) async-start(f32[8,2,4,48,256]{4,3,2,1,0:T(8,128)} %broadcast_select_fusion.4), calls=%async_computation.3 | async-start | bytes 6291456 | tf_op jit(solution)/shard_map/all_to_all | solution.py:10
  126.1 17.6 %collective-permute-start.9 = (f32[576,256]{1,0:T(8,128)S(1)}, f32[576,256]{1,0:T(8,128)}, u32[]{:S(2)}, u32[]{:S(2)}) collective-permute-start(f32[576,256]{1,0:T(8,128)S(1)} %collective-permute-done.7), channel_id=1, source_target_pairs={{8,0},{16,8},{9,1},{17,9},{10,2},{18,10},{11,3},{19,11},{12,4},{20... | collective-permute-start | bytes 1769480 | tf_op jit(solution)/shard_map/ppermute | solution.py:26
  162.5 41.5 %all-to-all-start.4 = ((f32[8,2,4,48,256]{4,3,2,1,0:T(8,128)}), f32[8,2,4,48,256]{4,3,2,1,0:T(8,128)S(1)}, u32[]{:S(2)}, u32[]{:S(2)}) async-start(f32[8,2,4,48,256]{4,3,2,1,0:T(8,128)} %broadcast_select_fusion.3), calls=%async_computation.4 | async-start | bytes 6291456 | tf_op jit(solution)/shard_map/all_to_all | solution.py:10
  170.2 17.9 %collective-permute-start.11 = (f32[576,256]{1,0:T(8,128)}, f32[576,256]{1,0:T(8,128)}, u32[]{:S(2)}, u32[]{:S(2)}) collective-permute-start(f32[576,256]{1,0:T(8,128)} %collective-permute-done.9), channel_id=1, source_target_pairs={{8,0},{9,1},{10,2},{11,3},{12,4},{13,5},{14,6},{15,7}} | collective-permute-start | bytes 1769480 | tf_op jit(solution)/shard_map/ppermute | solution.py:26
  216.3 42.3 %all-to-all-start.9 = ((f32[8,2,4,48,256]{4,3,2,1,0:T(8,128)}), f32[8,2,4,48,256]{4,3,2,1,0:T(8,128)}, u32[]{:S(2)}, u32[]{:S(2)}) async-start(f32[8,2,4,48,256]{4,3,2,1,0:T(8,128)} %broadcast_select_fusion), calls=%async_computation.9 | async-start | bytes 6291456 | tf_op jit(solution)/shard_map/all_to_all | solution.py:10
  258.7 42.6 %all-to-all-start.7 = ((f32[8,2,4,48,256]{4,3,2,1,0:T(8,128)}), f32[8,2,4,48,256]{4,3,2,1,0:T(8,128)}, u32[]{:S(2)}, u32[]{:S(2)}) async-start(f32[8,2,4,48,256]{4,3,2,1,0:T(8,128)} %broadcast_select_fusion.1), calls=%async_computation.7 | async-start | bytes 6291456 | tf_op jit(solution)/shard_map/all_to_all | solution.py:10
  301.2 43.2 %all-to-all-start.5 = ((f32[8,2,4,48,256]{4,3,2,1,0:T(8,128)}), f32[8,2,4,48,256]{4,3,2,1,0:T(8,128)}, u32[]{:S(2)}, u32[]{:S(2)}) async-start(f32[8,2,4,48,256]{4,3,2,1,0:T(8,128)} %broadcast_select_fusion.2), calls=%async_computation.5 | async-start | bytes 6291456 | tf_op jit(solution)/shard_map/all_to_all | solution.py:10
  344.4 42.5 %all-to-all-start.10 = ((f32[8,2,4,48,256]{4,3,2,1,0:T(8,128)}), f32[8,2,4,48,256]{4,3,2,1,0:T(8,128)}, u32[]{:S(2)}, u32[]{:S(2)}) async-start(f32[8,2,4,48,256]{4,3,2,1,0:T(8,128)} %copy.212), calls=%async_computation.10 | async-start | bytes 6291456 | tf_op jit(solution)/shard_map/all_to_all | solution.py:10
  386.9 42.6 %all-to-all-start.6 = ((f32[8,2,4,48,256]{4,3,2,1,0:T(8,128)}), f32[8,2,4,48,256]{4,3,2,1,0:T(8,128)}, u32[]{:S(2)}, u32[]{:S(2)}) async-start(f32[8,2,4,48,256]{4,3,2,1,0:T(8,128)} %copy.196), calls=%async_computation.6 | async-start | bytes 6291456 | tf_op jit(solution)/shard_map/all_to_all | solution.py:10
  429.5 42.4 %all-to-all-start.8 = ((f32[8,2,4,48,256]{4,3,2,1,0:T(8,128)}), f32[8,2,4,48,256]{4,3,2,1,0:T(8,128)}, u32[]{:S(2)}, u32[]{:S(2)}) async-start(f32[8,2,4,48,256]{4,3,2,1,0:T(8,128)} %copy.204), calls=%async_computation.8 | async-start | bytes 6291456 | tf_op jit(solution)/shard_map/all_to_all | solution.py:10
  483.5 42.5 %all-to-all-start.11 = ((f32[8,2,4,48,256]{4,3,2,1,0:T(8,128)}), f32[8,2,4,48,256]{4,3,2,1,0:T(8,128)}, u32[]{:S(2)}, u32[]{:S(2)}) async-start(f32[8,2,4,48,256]{4,3,2,1,0:T(8,128)} %copy.219), calls=%async_computation.11 | async-start | bytes 6291456 | tf_op jit(solution)/shard_map/all_to_all | solution.py:10
  497.9 14.6 %collective-permute-start.12 = (f32[12,48,256]{2,1,0:T(8,128)S(1)}, f32[12,48,256]{2,1,0:T(8,128)}, u32[]{:S(2)}, u32[]{:S(2)}) collective-permute-start(f32[12,48,256]{2,1,0:T(8,128)S(1)} %copy.217), channel_id=1, source_target_pairs={{0,8},{1,9},{2,10},{3,11},{4,12},{5,13},{6,14},{7,15}} | collective-permute-start | bytes 1769480 | tf_op jit(solution)/shard_map/ppermute | solution.py:57
  531.4 42.6 %all-to-all-start.12 = ((f32[8,2,4,48,256]{4,3,2,1,0:T(8,128)}), f32[8,2,4,48,256]{4,3,2,1,0:T(8,128)}, u32[]{:S(2)}, u32[]{:S(2)}) async-start(f32[8,2,4,48,256]{4,3,2,1,0:T(8,128)} %copy.224), calls=%async_computation.12 | async-start | bytes 6291456 | tf_op jit(solution)/shard_map/all_to_all | solution.py:10
  545.5 14.7 %collective-permute-start.14 = (f32[12,48,256]{2,1,0:T(8,128)S(1)}, f32[12,48,256]{2,1,0:T(8,128)}, u32[]{:S(2)}, u32[]{:S(2)}) collective-permute-start(f32[12,48,256]{2,1,0:T(8,128)S(1)} %copy.222), channel_id=1, source_target_pairs={{0,8},{8,16},{1,9},{9,17},{2,10},{10,18},{3,11},{11,19},{4,12},{12... | collective-permute-start | bytes 1769480 | tf_op jit(solution)/shard_map/ppermute | solution.py:57
  579.4 41.5 %all-to-all-start.13 = ((f32[8,2,4,48,256]{4,3,2,1,0:T(8,128)}), f32[8,2,4,48,256]{4,3,2,1,0:T(8,128)S(1)}, u32[]{:S(2)}, u32[]{:S(2)}) async-start(f32[8,2,4,48,256]{4,3,2,1,0:T(8,128)} %copy.229), calls=%async_computation.13 | async-start | bytes 6291456 | tf_op jit(solution)/shard_map/all_to_all | solution.py:10
  586.0 17.7 %collective-permute-start.17 = (f32[12,48,256]{2,1,0:T(8,128)S(1)}, f32[12,48,256]{2,1,0:T(8,128)S(1)}, u32[]{:S(2)}, u32[]{:S(2)}) collective-permute-start(f32[12,48,256]{2,1,0:T(8,128)S(1)} %copy.228), channel_id=1, source_target_pairs={{8,0},{16,8},{24,16},{9,1},{17,9},{25,17},{10,2},{18,10},{26,18},{... | collective-permute-start | bytes 1769480 | tf_op jit(solution)/shard_map/ppermute | solution.py:58
  587.3 17.4 %collective-permute-start.16 = (f32[12,48,256]{2,1,0:T(8,128)S(1)}, f32[12,48,256]{2,1,0:T(8,128)}, u32[]{:S(2)}, u32[]{:S(2)}) collective-permute-start(f32[12,48,256]{2,1,0:T(8,128)S(1)} %copy.227), channel_id=1, source_target_pairs={{0,8},{8,16},{16,24},{1,9},{9,17},{17,25},{2,10},{10,18},{18,26},{... | collective-permute-start | bytes 1769480 | tf_op jit(solution)/shard_map/ppermute | solution.py:57
  628.8 14.4 %collective-permute-start.21 = (f32[12,48,256]{2,1,0:T(8,128)S(1)}, f32[12,48,256]{2,1,0:T(8,128)S(1)}, u32[]{:S(2)}, u32[]{:S(2)}) collective-permute-start(f32[12,48,256]{2,1,0:T(8,128)S(1)} %copy.239), channel_id=1, source_target_pairs={{24,16},{25,17},{26,18},{27,19},{28,20},{29,21},{30,22},{31,23}} | collective-permute-start | bytes 1769480 | tf_op jit(solution)/shard_map/ppermute | solution.py:58
  643.6 14.9 %collective-permute-start.22 = (f32[12,48,256]{2,1,0:T(8,128)S(1)}, f32[12,48,256]{2,1,0:T(8,128)S(1)}, u32[]{:S(2)}, u32[]{:S(2)}) collective-permute-start(f32[12,48,256]{2,1,0:T(8,128)S(1)} %fusion.22), channel_id=1, source_target_pairs={{16,8},{24,16},{17,9},{25,17},{18,10},{26,18},{19,11},{27,19},{20,... | collective-permute-start | bytes 1769480 | tf_op jit(solution)/shard_map/ppermute | solution.py:58
  653.2 21.7 %collective-permute-start.20 = (f32[12,48,256]{2,1,0:T(8,128)}, f32[12,48,256]{2,1,0:T(8,128)}, u32[]{:S(2)}, u32[]{:S(2)}) collective-permute-start(f32[12,48,256]{2,1,0:T(8,128)} %fusion.23), channel_id=1, source_target_pairs={{0,8},{8,16},{16,24},{1,9},{9,17},{17,25},{2,10},{10,18},{18,26},{... | collective-permute-start | bytes 1769480 | tf_op jit(solution)/shard_map/ppermute | solution.py:57
  659.6 15.3 %collective-permute-start.23 = (f32[12,48,256]{2,1,0:T(8,128)}, f32[12,48,256]{2,1,0:T(8,128)}, u32[]{:S(2)}, u32[]{:S(2)}) collective-permute-start(f32[12,48,256]{2,1,0:T(8,128)} %fusion.21), channel_id=1, source_target_pairs={{8,0},{16,8},{24,16},{9,1},{17,9},{25,17},{10,2},{18,10},{26,18},{... | collective-permute-start | bytes 1769480 | tf_op jit(solution)/shard_map/ppermute | solution.py:58
  666.8 19.3 %all-to-all-start.14 = ((f32[576,8,32]{0,2,1:T(8,128)}), f32[576,8,32]{0,2,1:T(8,128)}, u32[]{:S(2)}, u32[]{:S(2)}) async-start(f32[576,8,32]{0,2,1:T(8,128)} %copy.259), calls=%async_computation.14 | async-start | bytes 1310720 | tf_op jit(solution)/shard_map/all_to_all | solution.py:149
  686.2 14.6 %all-to-all-start.15 = ((f32[576,8,32]{0,2,1:T(8,128)}), f32[576,8,32]{0,2,1:T(8,128)S(1)}, u32[]{:S(2)}, u32[]{:S(2)}) async-start(f32[576,8,32]{0,2,1:T(8,128)} %copy.260), calls=%async_computation.15 | async-start | bytes 1310720 | tf_op jit(solution)/shard_map/all_to_all | solution.py:149
  (69 other events, 657.8 us)
where the time goes:
time: 712 us; the launch traced here: 703 us
  waiting for transfers between devices  240 us (34%)
  local copies, waits for them, and re-layouts  151 us (21%)
  matrix products  128 us (18%)
  starting transfers between devices  117 us (16%)
  other arithmetic  45.7 us (6%)
  blocking collectives  16.1 us (2%)
    all_to_all x12, waiting for transfers between devices, band_exchange(): lax.all_to_all(outgoing, 'band', split_axis=0, concat_axis=0, tiled=True)  137 us
    all_to_all x12, starting transfers between devices, band_exchange(): lax.all_to_all(outgoing, 'band', split_axis=0, concat_axis=0, tiled=True)  53.2 us
    dot_general x6, matrix products, body(): jnp.dot(r[0], r[1].T, precision=PRECISION, preferred_element_type=jnp.flo...  52.3 us
    ppermute x6, waiting for transfers between devices, line_gather(): lax.ppermute(leftward, axis, [(i + 1, i) for i in range(0, count - step)])  51.8 us
    dot_general x6, matrix products, body(): jnp.dot(kernel, rows[h][1], precision=PRECISION, preferred_element_type=j...  43.4 us
    ppermute x6, waiting for transfers between devices, line_reduce(): lax.ppermute(send_right, axis, [(i, i + 1) for i in range(0, step)])  29.1 us
    dot_general x3, local copies, waits for them, and re-layouts, body(): jnp.dot(kernel.T, rows[h][0], precision=PRECISION, preferred_element_type...  28.9 us
    dot_general x6, matrix products, body(): jnp.dot(kernel.T, rows[h][0], precision=PRECISION, preferred_element_type...  27.7 us
  transfers between devices with their start and end apart: 39, of which 26 were waited for; matrix products, arithmetic and copies ran while one was open for 38% of the time, Pallas kernels for 0%

commit v1 on v0

--- a/solution.py
+++ b/solution.py
@@ -4,6 +4,29 @@
 from jax.sharding import PartitionSpec as P
 
 PRECISION = lax.Precision.HIGH
+
+
+def in_blocks(array, dim, size):
+    shape = array.shape
+    blocks = array.reshape(*shape[:dim], size, shape[dim] // size, *shape[dim + 1 :])
+    return jnp.moveaxis(blocks, dim, 0)
+
+
+def laid_out(pieces, dim):
+    shape = list(pieces.shape[1:])
+    shape[dim] *= pieces.shape[0]
+    return jnp.moveaxis(pieces, 0, dim).reshape(shape)
+
+
+def pairwise_exchange(x, axis, split_dim, concat_dim):
+    peers, index = (lax.axis_size(axis), lax.axis_index(axis))
+    pieces = in_blocks(x, split_dim, peers)
+    outs = [pieces[index]]
+    for hop in range(1, peers):
+        sent = pieces[index ^ hop]
+        outs.append(lax.ppermute(sent, axis, [(i, i ^ hop) for i in range(peers)]))
+    pieces = jnp.stack(outs)[index ^ jnp.arange(peers)]
+    return laid_out(pieces, concat_dim)
 
 
 def band_exchange(outgoing):
@@ -146,13 +169,7 @@
     first_home, second_returned = line_reduce(sum_blocks(returned[0]), "grp", group_count, held)
     second_home, _ = line_reduce(sum_blocks(second_returned), "grp", group_count)
     home = [
-        lax.all_to_all(
-            rows.reshape(block_count * piece_rows, half),
-            "band",
-            split_axis=1,
-            concat_axis=0,
-            tiled=True,
-        )
+        pairwise_exchange(rows.reshape(block_count * piece_rows, half), "band", 1, 0)
         for rows in (first_home, second_home)
     ]
     return jnp.concatenate(home, axis=1)

time: 712 us -> 756 us (1.062)
  local copies, waits for them, and re-layouts: 151 us -> 182 us
  starting transfers between devices: 117 us -> 128 us
    ppermute x0 -> x14, starting transfers between devices: none -> 22.4 us  [pairwise_exchange(): outs.append(lax.ppermute(sent, axis, [(i, i ^ hop) for i in range(peers)]))]
    unnamed x124 -> x162, local copies, waits for them, and re-layouts: 13.9 us -> 33 us
    another operation x4 -> x9, local copies, waits for them, and re-layouts: 2.58 us -> 21.3 us
    all_to_all x2 -> x0, waiting for transfers between devices: 14.8 us -> none  [body(): lax.all_to_all(rows.reshape(block_count * piece_rows, half), 'band', spli...]
    all_to_all x2 -> x0, starting transfers between devices: 11.6 us -> none  [body(): lax.all_to_all(rows.reshape(block_count * piece_rows, half), 'band', spli...]
    ppermute x0 -> x14, waiting for transfers between devices: none -> 9.02 us  [pairwise_exchange(): outs.append(lax.ppermute(sent, axis, [(i, i ^ hop) for i in range(peers)]))]
    all_to_all x8 -> x0, local copies, waits for them, and re-layouts: 8.82 us -> none  [body(): lax.all_to_all(rows.reshape(block_count * piece_rows, half), 'band', spli...]
  transfers between devices with their start and end apart: 39 -> 51, of which waited for: 26 -> 30; matrix products, arithmetic and copies ran while one was open for 38% -> 36% of each run, Pallas kernels for 0% -> 0%
where the time goes in v1:
time: 756 us; the launch traced here: 746 us
  waiting for transfers between devices  241 us (32%)
  local copies, waits for them, and re-layouts  182 us (24%)
  starting transfers between devices  128 us (17%)
  matrix products  128 us (17%)
  other arithmetic  45.8 us (6%)
  blocking collectives  16.1 us (2%)
    all_to_all x12, waiting for transfers between devices, band_exchange(): lax.all_to_all(outgoing, 'band', split_axis=0, concat_axis=0, tiled=True)  137 us
    all_to_all x12, starting transfers between devices, band_exchange(): lax.all_to_all(outgoing, 'band', split_axis=0, concat_axis=0, tiled=True)  53.2 us
    dot_general x6, matrix products, body(): jnp.dot(r[0], r[1].T, precision=PRECISION, preferred_element_type=jnp.flo...  52.3 us
    ppermute x6, waiting for transfers between devices, line_gather(): lax.ppermute(leftward, axis, [(i + 1, i) for i in range(0, count - step)])  52 us
    dot_general x6, matrix products, body(): jnp.dot(kernel, rows[h][1], precision=PRECISION, preferred_element_type=j...  43.4 us
    unnamed x162, local copies, waits for them, and re-layouts  33 us
    ppermute x6, waiting for transfers between devices, line_reduce(): lax.ppermute(send_right, axis, [(i, i + 1) for i in range(0, step)])  29.6 us
    dot_general x3, local copies, waits for them, and re-layouts, body(): jnp.dot(kernel.T, rows[h][0], precision=PRECISION, preferred_element_type...  29 us
  transfers between devices with their start and end apart: 51, of which 30 were waited for; matrix products, arithmetic and copies ran while one was open for 36% of the time, Pallas kernels for 0%

profile of v1, /device:TPU:0, one launch (start us, length us, event | category | flops | bytes accessed | tf_op | source)
XLA Modules:
  0.0 746.2 jit_solution(11628895938565403924)
XLA Ops:
  1.7 16.1 %all_to_all.98 = f32[8,576,32]{1,2,0:T(8,128)S(1)} all-to-all(f32[8,576,32]{1,2,0:T(8,128)S(1)} %copy.177), channel_id=1, replica_groups=mesh['grp'=4,'band'=8] {'band'}, dimensions={0} | all-to-all | bytes 1179648 | tf_op jit(solution)/shard_map/all_to_all | solution.py:103
  44.5 11.7 %collective-permute-done.3 = f32[576,256]{1,0:T(8,128)S(1)} collective-permute-done((f32[576,256]{1,0:T(8,128)}, f32[576,256]{1,0:T(8,128)S(1)}, u32[]{:S(2)}, u32[]{:S(2)}) %collective-permute-start.3) | collective-permute-done | bytes 589856 | tf_op jit(solution)/shard_map/ppermute | solution.py:49
  57.6 13.5 %collective-permute-done.5 = f32[576,256]{1,0:T(8,128)S(1)} collective-permute-done((f32[576,256]{1,0:T(8,128)S(1)}, f32[576,256]{1,0:T(8,128)S(1)}, u32[]{:S(2)}, u32[]{:S(2)}) %collective-permute-start.5) | collective-permute-done | bytes 589856 | tf_op jit(solution)/shard_map/ppermute | solution.py:49
  103.4 16.7 %all-to-all-done.2 = f32[8,2,4,48,256]{4,3,2,1,0:T(8,128)} async-done(((f32[8,2,4,48,256]{4,3,2,1,0:T(8,128)}), f32[8,2,4,48,256]{4,3,2,1,0:T(8,128)}, u32[]{:S(2)}, u32[]{:S(2)}) %all-to-all-start.2) | async-done | bytes 3145760 | tf_op jit(solution)/shard_map/all_to_all | solution.py:33
  136.3 7.4 collective-permute-done.9
  143.7 18.8 %all-to-all-done.3 = f32[8,2,4,48,256]{4,3,2,1,0:T(8,128)} async-done(((f32[8,2,4,48,256]{4,3,2,1,0:T(8,128)}), f32[8,2,4,48,256]{4,3,2,1,0:T(8,128)}, u32[]{:S(2)}, u32[]{:S(2)}) %all-to-all-start.3) | async-done | bytes 3145760 | tf_op jit(solution)/shard_map/all_to_all | solution.py:33
  176.3 11.8 %collective-permute-done.11 = f32[576,256]{1,0:T(8,128)} collective-permute-done((f32[576,256]{1,0:T(8,128)}, f32[576,256]{1,0:T(8,128)}, u32[]{:S(2)}, u32[]{:S(2)}) %collective-permute-start.11) | collective-permute-done | bytes 589856 | tf_op jit(solution)/shard_map/ppermute | solution.py:49
  188.1 15.8 %all-to-all-done.4 = f32[8,2,4,48,256]{4,3,2,1,0:T(8,128)S(1)} async-done(((f32[8,2,4,48,256]{4,3,2,1,0:T(8,128)}), f32[8,2,4,48,256]{4,3,2,1,0:T(8,128)S(1)}, u32[]{:S(2)}, u32[]{:S(2)}) %all-to-all-start.4) | async-done | bytes 3145760 | tf_op jit(solution)/shard_map/all_to_all | solution.py:33
  231.8 27.0 %all-to-all-done.9 = f32[8,2,4,48,256]{4,3,2,1,0:T(8,128)} async-done(((f32[8,2,4,48,256]{4,3,2,1,0:T(8,128)}), f32[8,2,4,48,256]{4,3,2,1,0:T(8,128)}, u32[]{:S(2)}, u32[]{:S(2)}) %all-to-all-start.9) | async-done | bytes 3145760 | tf_op jit(solution)/shard_map/all_to_all | solution.py:33
  265.9 6.4 fusion.45
  291.2 6.4 fusion.47
  312.0 9.6 %fusion = f32[1536,1536]{1,0:T(8,128)} fusion(f32[1536,1536]{1,0:T(8,128)S(1)} %copy-done.5, f32[1536,256]{1,0:T(8,128)S(1)} %bitcast.387, f32[1536,256]{1,0:T(8,128)S(1)} %bitcast.389, f32[3,1536,1536]{2,1,0:T(8,128)} %param.7, f32[]{:T(128)} %bitcast.81), kind=kOutput, calls=%fused_computation.9 | convolution fusion | flops 3630956544 | bytes 31457284 | tf_op jit(solution)/shard_map/dot_general | solution.py:143
  321.6 9.7 %copy.211 = f32[1536,1536]{1,0:T(8,128)} copy(f32[1536,1536]{0,1:T(8,128)} %bitcast.356) | data formatting | bytes 18874368 | tf_op jit(solution)/shard_map/dot_general | solution.py:153
  331.2 7.0 convolution_bitcast_fusion.7
  351.7 12.1 %fusion.2 = f32[1536,1536]{1,0:T(8,128)} fusion(f32[1536,1536]{1,0:T(8,128)} %fusion.45, f32[1536,256]{1,0:T(8,128)S(1)} %bitcast.397, f32[1536,256]{1,0:T(8,128)S(1)} %bitcast.395, f32[3,1536,1536]{2,1,0:T(8,128)} %param.7, f32[]{:T(128)} %bitcast.39), kind=kOutput, calls=%fused_computation.13 | convolution fusion | flops 3630956544 | bytes 31457284 | tf_op jit(solution)/shard_map/dot_general | solution.py:143
  363.8 9.7 %copy.195 = f32[1536,1536]{1,0:T(8,128)} copy(f32[1536,1536]{0,1:T(8,128)} %bitcast.362) | data formatting | bytes 18874368 | tf_op jit(solution)/shard_map/dot_general | solution.py:153
  373.5 7.0 convolution_bitcast_fusion.11
  394.2 11.4 %fusion.1 = f32[1536,1536]{1,0:T(8,128)} fusion(f32[1536,1536]{1,0:T(8,128)} %fusion.46, f32[1536,256]{1,0:T(8,128)S(1)} %bitcast.391, f32[1536,256]{1,0:T(8,128)S(1)} %bitcast.393, f32[3,1536,1536]{2,1,0:T(8,128)} %param.7, f32[]{:T(128)} %bitcast.60), kind=kOutput, calls=%fused_computation.11 | convolution fusion | flops 3630956544 | bytes 31457284 | tf_op jit(solution)/shard_map/dot_general | solution.py:143
  405.6 9.6 %copy.203 = f32[1536,1536]{1,0:T(8,128)} copy(f32[1536,1536]{0,1:T(8,128)} %bitcast.359) | data formatting | bytes 18874368 | tf_op jit(solution)/shard_map/dot_general | solution.py:153
  415.3 7.4 convolution_bitcast_fusion.9
  434.2 7.4 convolution_bitcast_fusion.5
  441.6 7.3 convolution_bitcast_fusion.4
  461.7 10.3 %all-to-all-done.8 = f32[8,2,4,48,256]{4,3,2,1,0:T(8,128)} async-done(((f32[8,2,4,48,256]{4,3,2,1,0:T(8,128)}), f32[8,2,4,48,256]{4,3,2,1,0:T(8,128)}, u32[]{:S(2)}, u32[]{:S(2)}) %all-to-all-start.8) | async-done | bytes 3145760 | tf_op jit(solution)/shard_map/all_to_all | solution.py:33
  488.4 7.5 convolution_bitcast_fusion.3
  512.7 13.5 %all-to-all-done.11 = f32[8,2,4,48,256]{4,3,2,1,0:T(8,128)} async-done(((f32[8,2,4,48,256]{4,3,2,1,0:T(8,128)}), f32[8,2,4,48,256]{4,3,2,1,0:T(8,128)}, u32[]{:S(2)}, u32[]{:S(2)}) %all-to-all-start.11) | async-done | bytes 3145760 | tf_op jit(solution)/shard_map/all_to_all | solution.py:33
  536.4 7.0 convolution_bitcast_fusion.1
  554.0 6.3 collective-permute-done.14
  560.3 13.9 %all-to-all-done.12 = f32[8,2,4,48,256]{4,3,2,1,0:T(8,128)} async-done(((f32[8,2,4,48,256]{4,3,2,1,0:T(8,128)}), f32[8,2,4,48,256]{4,3,2,1,0:T(8,128)}, u32[]{:S(2)}, u32[]{:S(2)}) %all-to-all-start.12) | async-done | bytes 3145760 | tf_op jit(solution)/shard_map/all_to_all | solution.py:33
  605.0 16.1 %all-to-all-done.13 = f32[8,2,4,48,256]{4,3,2,1,0:T(8,128)S(1)} async-done(((f32[8,2,4,48,256]{4,3,2,1,0:T(8,128)}), f32[8,2,4,48,256]{4,3,2,1,0:T(8,128)S(1)}, u32[]{:S(2)}, u32[]{:S(2)}) %all-to-all-start.13) | async-done | bytes 3145760 | tf_op jit(solution)/shard_map/all_to_all | solution.py:33
  629.8 8.7 %collective-permute-done.25 = f32[12,48,256]{2,1,0:T(8,128)S(1)} collective-permute-done((f32[12,48,256]{2,1,0:T(8,128)S(1)}, f32[12,48,256]{2,1,0:T(8,128)S(1)}, u32[]{:S(2)}, u32[]{:S(2)}) %collective-permute-start.25) | collective-permute-done | bytes 589856 | tf_op jit(solution)/shard_map/ppermute | solution.py:80
  644.5 7.6 %collective-permute-done.26 = f32[12,48,256]{2,1,0:T(8,128)S(1)} collective-permute-done((f32[12,48,256]{2,1,0:T(8,128)S(1)}, f32[12,48,256]{2,1,0:T(8,128)S(1)}, u32[]{:S(2)}, u32[]{:S(2)}) %collective-permute-start.26) | collective-permute-done | bytes 589856 | tf_op jit(solution)/shard_map/ppermute | solution.py:80
  677.5 13.3 %constant_dynamic-slice_fusion = (f32[576,1,32]{2,1,0:T(1,128)}, f32[576,1,32]{2,1,0:T(1,128)}, f32[576,1,32]{2,1,0:T(1,128)}, f32[576,1,32]{2,1,0:T(1,128)}, f3...) fusion(f32[576,8,32]{2,1,0:T(8,128)} %reshape.348, ...), kind=kLoop, calls=%fused_computation.107 | loop fusion | bytes 2359328 | tf_op jit(solution)/shard_map/dynamic-slice.29
  (382 shorter events, 386.0 us)
Async XLA Ops:
  18.8 16.2 %collective-permute-start = (f32[576,256]{1,0:T(8,128)}, f32[576,256]{1,0:T(8,128)}, u32[]{:S(2)}, u32[]{:S(2)}) collective-permute-start(f32[576,256]{1,0:T(8,128)} %copy.179), channel_id=1, source_target_pairs={{0,8},{8,16},{16,24},{1,9},{9,17},{17,25},{2,10},{10,18},{18,26},{... | collective-permute-start | bytes 1769480 | tf_op jit(solution)/shard_map/ppermute | solution.py:48
  23.1 16.8 %collective-permute-start.1 = (f32[576,256]{1,0:T(8,128)}, f32[576,256]{1,0:T(8,128)}, u32[]{:S(2)}, u32[]{:S(2)}) collective-permute-start(f32[576,256]{1,0:T(8,128)} %copy.179), channel_id=1, source_target_pairs={{8,0},{16,8},{24,16},{9,1},{17,9},{25,17},{10,2},{18,10},{26,18},{... | collective-permute-start | bytes 1769480 | tf_op jit(solution)/shard_map/ppermute | solution.py:49
  25.6 52.2 %all-to-all-start = ((f32[8,576,32]{1,2,0:T(8,128)}), f32[8,576,32]{1,2,0:T(8,128)S(1)}, u32[]{:S(2)}, u32[]{:S(2)}) async-start(f32[8,576,32]{1,2,0:T(8,128)} %copy.175), calls=%async_computation | async-start | bytes 1310720 | tf_op jit(solution)/shard_map/all_to_all | solution.py:103
  39.9 16.2 %collective-permute-start.3 = (f32[576,256]{1,0:T(8,128)}, f32[576,256]{1,0:T(8,128)S(1)}, u32[]{:S(2)}, u32[]{:S(2)}) collective-permute-start(f32[576,256]{1,0:T(8,128)} %collective-permute-done.1), channel_id=1, source_target_pairs={{8,0},{16,8},{9,1},{17,9},{10,2},{18,10},{11,3},{19,11},{12,4},{20... | collective-permute-start | bytes 1769480 | tf_op jit(solution)/shard_map/ppermute | solution.py:49
  42.7 14.9 %collective-permute-start.4 = (f32[576,256]{1,0:T(8,128)S(1)}, f32[576,256]{1,0:T(8,128)S(1)}, u32[]{:S(2)}, u32[]{:S(2)}) collective-permute-start(f32[576,256]{1,0:T(8,128)S(1)} %collective-permute-done.2), channel_id=1, source_target_pairs={{16,24},{17,25},{18,26},{19,27},{20,28},{21,29},{22,30},{23,31}} | collective-permute-start | bytes 1769480 | tf_op jit(solution)/shard_map/ppermute | solution.py:48
  56.2 14.9 %collective-permute-start.5 = (f32[576,256]{1,0:T(8,128)S(1)}, f32[576,256]{1,0:T(8,128)S(1)}, u32[]{:S(2)}, u32[]{:S(2)}) collective-permute-start(f32[576,256]{1,0:T(8,128)S(1)} %collective-permute-done.3), channel_id=1, source_target_pairs={{8,0},{9,1},{10,2},{11,3},{12,4},{13,5},{14,6},{15,7}} | collective-permute-start | bytes 1769480 | tf_op jit(solution)/shard_map/ppermute | solution.py:49
  77.8 42.3 %all-to-all-start.2 = ((f32[8,2,4,48,256]{4,3,2,1,0:T(8,128)}), f32[8,2,4,48,256]{4,3,2,1,0:T(8,128)}, u32[]{:S(2)}, u32[]{:S(2)}) async-start(f32[8,2,4,48,256]{4,3,2,1,0:T(8,128)} %broadcast_select_fusion.5), calls=%async_computation.2 | async-start | bytes 6291456 | tf_op jit(solution)/shard_map/all_to_all | solution.py:33
  84.4 17.7 %collective-permute-start.7 = (f32[576,256]{1,0:T(8,128)}, f32[576,256]{1,0:T(8,128)S(1)}, u32[]{:S(2)}, u32[]{:S(2)}) collective-permute-start(f32[576,256]{1,0:T(8,128)} %copy.183), channel_id=1, source_target_pairs={{8,0},{16,8},{24,16},{9,1},{17,9},{25,17},{10,2},{18,10},{26,18},{... | collective-permute-start | bytes 1769480 | tf_op jit(solution)/shard_map/ppermute | solution.py:49
  85.7 17.7 %collective-permute-start.6 = (f32[576,256]{1,0:T(8,128)}, f32[576,256]{1,0:T(8,128)S(1)}, u32[]{:S(2)}, u32[]{:S(2)}) collective-permute-start(f32[576,256]{1,0:T(8,128)} %copy.182), channel_id=1, source_target_pairs={{0,8},{8,16},{16,24},{1,9},{9,17},{17,25},{2,10},{10,18},{18,26},{... | collective-permute-start | bytes 1769480 | tf_op jit(solution)/shard_map/ppermute | solution.py:48
  120.1 42.4 %all-to-all-start.3 = ((f32[8,2,4,48,256]{4,3,2,1,0:T(8,128)}), f32[8,2,4,48,256]{4,3,2,1,0:T(8,128)}, u32[]{:S(2)}, u32[]{:S(2)}) async-start(f32[8,2,4,48,256]{4,3,2,1,0:T(8,128)} %broadcast_select_fusion.4), calls=%async_computation.3 | async-start | bytes 6291456 | tf_op jit(solution)/shard_map/all_to_all | solution.py:33
  126.1 17.6 %collective-permute-start.9 = (f32[576,256]{1,0:T(8,128)S(1)}, f32[576,256]{1,0:T(8,128)}, u32[]{:S(2)}, u32[]{:S(2)}) collective-permute-start(f32[576,256]{1,0:T(8,128)S(1)} %collective-permute-done.7), channel_id=1, source_target_pairs={{8,0},{16,8},{9,1},{17,9},{10,2},{18,10},{11,3},{19,11},{12,4},{20... | collective-permute-start | bytes 1769480 | tf_op jit(solution)/shard_map/ppermute | solution.py:49
  162.5 41.5 %all-to-all-start.4 = ((f32[8,2,4,48,256]{4,3,2,1,0:T(8,128)}), f32[8,2,4,48,256]{4,3,2,1,0:T(8,128)S(1)}, u32[]{:S(2)}, u32[]{:S(2)}) async-start(f32[8,2,4,48,256]{4,3,2,1,0:T(8,128)} %broadcast_select_fusion.3), calls=%async_computation.4 | async-start | bytes 6291456 | tf_op jit(solution)/shard_map/all_to_all | solution.py:33
  170.3 17.9 %collective-permute-start.11 = (f32[576,256]{1,0:T(8,128)}, f32[576,256]{1,0:T(8,128)}, u32[]{:S(2)}, u32[]{:S(2)}) collective-permute-start(f32[576,256]{1,0:T(8,128)} %collective-permute-done.9), channel_id=1, source_target_pairs={{8,0},{9,1},{10,2},{11,3},{12,4},{13,5},{14,6},{15,7}} | collective-permute-start | bytes 1769480 | tf_op jit(solution)/shard_map/ppermute | solution.py:49
  216.4 42.4 %all-to-all-start.9 = ((f32[8,2,4,48,256]{4,3,2,1,0:T(8,128)}), f32[8,2,4,48,256]{4,3,2,1,0:T(8,128)}, u32[]{:S(2)}, u32[]{:S(2)}) async-start(f32[8,2,4,48,256]{4,3,2,1,0:T(8,128)} %broadcast_select_fusion), calls=%async_computation.9 | async-start | bytes 6291456 | tf_op jit(solution)/shard_map/all_to_all | solution.py:33
  258.7 42.6 %all-to-all-start.7 = ((f32[8,2,4,48,256]{4,3,2,1,0:T(8,128)}), f32[8,2,4,48,256]{4,3,2,1,0:T(8,128)}, u32[]{:S(2)}, u32[]{:S(2)}) async-start(f32[8,2,4,48,256]{4,3,2,1,0:T(8,128)} %broadcast_select_fusion.1), calls=%async_computation.7 | async-start | bytes 6291456 | tf_op jit(solution)/shard_map/all_to_all | solution.py:33
  301.3 43.3 %all-to-all-start.5 = ((f32[8,2,4,48,256]{4,3,2,1,0:T(8,128)}), f32[8,2,4,48,256]{4,3,2,1,0:T(8,128)}, u32[]{:S(2)}, u32[]{:S(2)}) async-start(f32[8,2,4,48,256]{4,3,2,1,0:T(8,128)} %broadcast_select_fusion.2), calls=%async_computation.5 | async-start | bytes 6291456 | tf_op jit(solution)/shard_map/all_to_all | solution.py:33
  344.6 42.5 %all-to-all-start.10 = ((f32[8,2,4,48,256]{4,3,2,1,0:T(8,128)}), f32[8,2,4,48,256]{4,3,2,1,0:T(8,128)}, u32[]{:S(2)}, u32[]{:S(2)}) async-start(f32[8,2,4,48,256]{4,3,2,1,0:T(8,128)} %copy.212), calls=%async_computation.10 | async-start | bytes 6291456 | tf_op jit(solution)/shard_map/all_to_all | solution.py:33
  387.1 42.6 %all-to-all-start.6 = ((f32[8,2,4,48,256]{4,3,2,1,0:T(8,128)}), f32[8,2,4,48,256]{4,3,2,1,0:T(8,128)}, u32[]{:S(2)}, u32[]{:S(2)}) async-start(f32[8,2,4,48,256]{4,3,2,1,0:T(8,128)} %copy.196), calls=%async_computation.6 | async-start | bytes 6291456 | tf_op jit(solution)/shard_map/all_to_all | solution.py:33
  429.7 42.4 %all-to-all-start.8 = ((f32[8,2,4,48,256]{4,3,2,1,0:T(8,128)}), f32[8,2,4,48,256]{4,3,2,1,0:T(8,128)}, u32[]{:S(2)}, u32[]{:S(2)}) async-start(f32[8,2,4,48,256]{4,3,2,1,0:T(8,128)} %copy.204), calls=%async_computation.8 | async-start | bytes 6291456 | tf_op jit(solution)/shard_map/all_to_all | solution.py:33
  483.7 42.5 %all-to-all-start.11 = ((f32[8,2,4,48,256]{4,3,2,1,0:T(8,128)}), f32[8,2,4,48,256]{4,3,2,1,0:T(8,128)}, u32[]{:S(2)}, u32[]{:S(2)}) async-start(f32[8,2,4,48,256]{4,3,2,1,0:T(8,128)} %copy.219), calls=%async_computation.11 | async-start | bytes 6291456 | tf_op jit(solution)/shard_map/all_to_all | solution.py:33
  498.0 14.6 %collective-permute-start.12 = (f32[12,48,256]{2,1,0:T(8,128)S(1)}, f32[12,48,256]{2,1,0:T(8,128)}, u32[]{:S(2)}, u32[]{:S(2)}) collective-permute-start(f32[12,48,256]{2,1,0:T(8,128)S(1)} %copy.217), channel_id=1, source_target_pairs={{0,8},{1,9},{2,10},{3,11},{4,12},{5,13},{6,14},{7,15}} | collective-permute-start | bytes 1769480 | tf_op jit(solution)/shard_map/ppermute | solution.py:80
  531.6 42.6 %all-to-all-start.12 = ((f32[8,2,4,48,256]{4,3,2,1,0:T(8,128)}), f32[8,2,4,48,256]{4,3,2,1,0:T(8,128)}, u32[]{:S(2)}, u32[]{:S(2)}) async-start(f32[8,2,4,48,256]{4,3,2,1,0:T(8,128)} %copy.224), calls=%async_computation.12 | async-start | bytes 6291456 | tf_op jit(solution)/shard_map/all_to_all | solution.py:33
  545.7 14.7 %collective-permute-start.14 = (f32[12,48,256]{2,1,0:T(8,128)S(1)}, f32[12,48,256]{2,1,0:T(8,128)}, u32[]{:S(2)}, u32[]{:S(2)}) collective-permute-start(f32[12,48,256]{2,1,0:T(8,128)S(1)} %copy.222), channel_id=1, source_target_pairs={{0,8},{8,16},{1,9},{9,17},{2,10},{10,18},{3,11},{11,19},{4,12},{12... | collective-permute-start | bytes 1769480 | tf_op jit(solution)/shard_map/ppermute | solution.py:80
  579.7 41.5 %all-to-all-start.13 = ((f32[8,2,4,48,256]{4,3,2,1,0:T(8,128)}), f32[8,2,4,48,256]{4,3,2,1,0:T(8,128)S(1)}, u32[]{:S(2)}, u32[]{:S(2)}) async-start(f32[8,2,4,48,256]{4,3,2,1,0:T(8,128)} %copy.229), calls=%async_computation.13 | async-start | bytes 6291456 | tf_op jit(solution)/shard_map/all_to_all | solution.py:33
  586.3 17.7 %collective-permute-start.17 = (f32[12,48,256]{2,1,0:T(8,128)S(1)}, f32[12,48,256]{2,1,0:T(8,128)S(1)}, u32[]{:S(2)}, u32[]{:S(2)}) collective-permute-start(f32[12,48,256]{2,1,0:T(8,128)S(1)} %copy.228), channel_id=1, source_target_pairs={{8,0},{16,8},{24,16},{9,1},{17,9},{25,17},{10,2},{18,10},{26,18},{... | collective-permute-start | bytes 1769480 | tf_op jit(solution)/shard_map/ppermute | solution.py:81
  587.6 17.4 %collective-permute-start.16 = (f32[12,48,256]{2,1,0:T(8,128)S(1)}, f32[12,48,256]{2,1,0:T(8,128)}, u32[]{:S(2)}, u32[]{:S(2)}) collective-permute-start(f32[12,48,256]{2,1,0:T(8,128)S(1)} %copy.227), channel_id=1, source_target_pairs={{0,8},{8,16},{16,24},{1,9},{9,17},{17,25},{2,10},{10,18},{18,26},{... | collective-permute-start | bytes 1769480 | tf_op jit(solution)/shard_map/ppermute | solution.py:80
  629.0 14.2 %collective-permute-start.28 = (f32[12,48,256]{2,1,0:T(8,128)S(1)}, f32[12,48,256]{2,1,0:T(8,128)S(1)}, u32[]{:S(2)}, u32[]{:S(2)}) collective-permute-start(f32[12,48,256]{2,1,0:T(8,128)S(1)} %copy.239), channel_id=1, source_target_pairs={{24,16},{25,17},{26,18},{27,19},{28,20},{29,21},{30,22},{31,23}} | collective-permute-start | bytes 1769480 | tf_op jit(solution)/shard_map/ppermute | solution.py:81
  643.7 14.9 %collective-permute-start.29 = (f32[12,48,256]{2,1,0:T(8,128)S(1)}, f32[12,48,256]{2,1,0:T(8,128)S(1)}, u32[]{:S(2)}, u32[]{:S(2)}) collective-permute-start(f32[12,48,256]{2,1,0:T(8,128)S(1)} %fusion.22), channel_id=1, source_target_pairs={{16,8},{24,16},{17,9},{25,17},{18,10},{26,18},{19,11},{27,19},{20,... | collective-permute-start | bytes 1769480 | tf_op jit(solution)/shard_map/ppermute | solution.py:81
  701.8 31.9 %collective-permute-start.24 = (f32[576,32]{0,1:T(8,128)}, f32[576,32]{0,1:T(8,128)}, u32[]{:S(2)}, u32[]{:S(2)}) collective-permute-start(f32[576,32]{0,1:T(8,128)} %bitcast.145), channel_id=1, source_target_pairs={{0,7},{1,6},{2,5},{3,4},{4,3},{5,2},{6,1},{7,0},{8,15},{9,14},{10,... | collective-permute-start | bytes 221192 | tf_op jit(solution)/shard_map/ppermute | solution.py:27
  707.3 25.0 %collective-permute-start.23 = (f32[576,32]{0,1:T(8,128)}, f32[576,32]{0,1:T(8,128)}, u32[]{:S(2)}, u32[]{:S(2)}) collective-permute-start(f32[576,32]{0,1:T(8,128)} %bitcast.143), channel_id=1, source_target_pairs={{0,6},{1,7},{2,4},{3,5},{4,2},{5,3},{6,0},{7,1},{8,14},{9,15},{10,... | collective-permute-start | bytes 221192 | tf_op jit(solution)/shard_map/ppermute | solution.py:27
  710.9 20.3 %collective-permute-start.22 = (f32[576,32]{0,1:T(8,128)}, f32[576,32]{0,1:T(8,128)}, u32[]{:S(2)}, u32[]{:S(2)}) collective-permute-start(f32[576,32]{0,1:T(8,128)} %bitcast.141), channel_id=1, source_target_pairs={{0,5},{1,4},{2,7},{3,6},{4,1},{5,0},{6,3},{7,2},{8,13},{9,12},{10,... | collective-permute-start | bytes 221192 | tf_op jit(solution)/shard_map/ppermute | solution.py:27
  713.0 15.5 %collective-permute-start.21 = (f32[576,32]{0,1:T(8,128)}, f32[576,32]{0,1:T(8,128)}, u32[]{:S(2)}, u32[]{:S(2)}) collective-permute-start(f32[576,32]{0,1:T(8,128)} %bitcast.139), channel_id=1, source_target_pairs={{0,4},{1,5},{2,6},{3,7},{4,0},{5,1},{6,2},{7,3},{8,12},{9,13},{10,... | collective-permute-start | bytes 221192 | tf_op jit(solution)/shard_map/ppermute | solution.py:27
  (85 other events, 820.1 us)
